TPU v7x, 256 devices: a whole 4x4x8 slice. The times are simulated.
256 devices in a mesh: seq: 32 (over z, x_hi, core), mp: 8 (over x_lo, y).
Axes of the slice: x: 4 (x_hi: 2, x_lo: 2; x = x_hi * 2 + x_lo), y: 4, z: 8, core: 2. Of those that a mesh axis runs over, the one named last changes fastest.
Arguments:
- queries: bfloat16 [4096, 8192], P('seq', 'mp'), may hold values from -200 to 200
- keys: bfloat16 [4096, 1024], P('seq', 'mp'), may hold values from -7 to 7
- values: float32 [4096, 1024], P('seq', 'mp'), may hold values from -24 to 24
- inputs_x: bfloat16 [4096, 8192], P('seq', 'mp'), may hold values from -6 to 6
- in_b: bfloat16 [4096, 128], P('seq'), may hold values from -6 to 6
- in_c: bfloat16 [4096, 128], P('seq'), may hold values from -6 to 6
- log_decay: float32 [4096, 64], P('seq', 'mp'), may hold values from -2 to 0
Outputs:
- grad_x: float32 [4096, 8192], P('seq', 'mp')
- grad_b: float32 [4096, 128], P(('seq', 'mp'))
- grad_c: float32 [4096, 128], P(('seq', 'mp'))
All inputs are finite; a program needn't handle non-finite values.
Results may differ from a plain program's by a relative error of at most 0.00035.
Values may be sent and summed in bfloat16 or wider, within the bound.
No kernel may reach another device: no remote copies, remote signals or barrier semaphores. Data moves between devices by JAX's collectives and lax.ppermute only.
A program may use at most 128 MiB of HBM per device.

v0:
```python
import math
import jax
import jax.numpy as jnp
from jax import lax
from jax.sharding import PartitionSpec as P

HEAD_WIDTH = 128
N = 128
HQ_DEV = 8
KV_DEV = 1
very_negative = -1e30
highest = lax.Precision.HIGHEST


def prefix(value, axis, join, neutral):
    count, mine = (lax.axis_size(axis), lax.axis_index(axis))
    pieces = jax.tree.map(lambda part: lax.all_gather(part, axis), value)
    subtotal = jax.tree.map(
        lambda part, zero: jnp.full_like(part, 0) + jnp.asarray(zero, part.dtype), value, neutral
    )

    def hop(position, subtotal):
        longer = join(subtotal, jax.tree.map(lambda part: part[position], pieces))
        return jax.tree.map(lambda new, old: jnp.where(position < mine, new, old), longer, subtotal)

    return lax.fori_loop(0, count - 1, hop, subtotal)


def chain_step(earlier, later):
    return (earlier[0] + later[0], jnp.exp(later[0])[:, None, None] * earlier[1] + later[1])


def attend_rows(current, query_head_rows, query_pos, key_piece, value_piece):
    row_top, denominator, mixture = current
    piece_rows = key_piece.shape[0]
    kv_heads = query_head_rows.shape[1]
    key_head_rows = key_piece.reshape(piece_rows, kv_heads, HEAD_WIDTH)
    value_head_rows = value_piece.reshape(piece_rows, kv_heads, HEAD_WIDTH)
    scores = jnp.einsum(
        "qkgd,nkd->qkgn", query_head_rows, key_head_rows, precision=highest
    ) / math.sqrt(HEAD_WIDTH)
    key_pos = jnp.arange(piece_rows, dtype=jnp.int32)
    allowed = (key_pos[None, :] <= query_pos[:, None])[:, None, None, :]
    scores = jnp.where(allowed, scores, very_negative)
    new_top = jnp.maximum(row_top, jnp.max(scores, axis=-1))
    weights = jnp.where(allowed, jnp.exp(scores - new_top[..., None]), 0.0)
    denominator = jnp.sum(weights, axis=-1)
    mixture = jnp.einsum("qkgn,nkd->qkgd", weights, value_head_rows, precision=highest)
    return (new_top, denominator, mixture)


def local(queries, keys, values, inputs_x, in_b, in_c, log_decay):
    row_count = queries.shape[0]
    group_width = HQ_DEV // KV_DEV
    seq_count = lax.axis_size("seq")
    own_index = lax.axis_index("seq")
    first_query = own_index * row_count
    query_sets = ((queries, first_query + jnp.arange(row_count, dtype=jnp.int32)),)
    head_sets = tuple(
        (
            rows.astype(jnp.float32).reshape(rows.shape[0], KV_DEV, group_width, HEAD_WIDTH)
            for rows, positions in query_sets
        )
    )
    pos_sets = tuple((positions for rows, positions in query_sets))
    start_state = tuple(
        (
            (
                jnp.full((positions.shape[0], KV_DEV, group_width), very_negative, jnp.float32),
                jnp.zeros((positions.shape[0], KV_DEV, group_width), jnp.float32),
                jnp.zeros((positions.shape[0], KV_DEV, group_width, HEAD_WIDTH), jnp.float32),
            )
            for positions in pos_sets
        )
    )
    key_piece = lax.all_gather(keys.astype(jnp.float32), "seq", axis=0, tiled=True)
    value_piece = lax.all_gather(values, "seq", axis=0, tiled=True)
    updated = []
    for current, query_head_rows, query_pos in zip(start_state, head_sets, pos_sets):

        def compute(state_now, query_head_rows=query_head_rows, query_pos=query_pos):
            return attend_rows(state_now, query_head_rows, query_pos, key_piece, value_piece)

        updated.append(compute(current))
    finished = tuple(updated)
    outputs = [
        (mixture / denominator[..., None]).reshape(mixture.shape[0], HQ_DEV, HEAD_WIDTH)
        for row_top, denominator, mixture in finished
    ]
    teacher_out = outputs[0]
    c_scale = 0.5 / math.sqrt(N * row_count * seq_count)
    student_x = inputs_x.astype(jnp.float32).reshape(row_count, HQ_DEV, HEAD_WIDTH)
    b_rows = in_b.astype(jnp.float32)
    c_rows = in_c.astype(jnp.float32) * c_scale
    cumulative = jnp.cumsum(log_decay, axis=0)
    totals = cumulative[-1]
    heads_first = cumulative.T
    causal = jnp.arange(row_count)[:, None] >= jnp.arange(row_count)[None, :]
    decays = jnp.exp(
        jnp.where(causal[None], heads_first[:, :, None] - heads_first[:, None, :], -jnp.inf)
    )
    inner_products = jnp.dot(in_c, in_b.T, preferred_element_type=jnp.float32) * c_scale
    mixing = decays * inner_products[None]
    rising = jnp.exp(cumulative)
    ending = jnp.exp(totals[None, :] - cumulative)
    local_state = jnp.einsum(
        "shp,sn->hpn", student_x * ending[:, :, None], b_rows, precision=highest
    )
    identity = (jnp.zeros_like(totals), jnp.zeros_like(local_state))
    prefix_log, state_in = prefix((totals, local_state), "seq", chain_step, identity)
    y_intra = jnp.einsum("hts,shp->thp", mixing, student_x, precision=highest)
    y_inter = jnp.einsum("tn,hpn->thp", c_rows, state_in, precision=highest) * rising[:, :, None]
    mismatch = y_intra + y_inter - teacher_out
    scaled_mismatch = mismatch * rising[:, :, None]
    local_grad = jnp.einsum("thp,tn->hpn", scaled_mismatch, c_rows, precision=highest)
    grad_pieces = lax.all_gather(local_grad[None], "seq", axis=0, tiled=True)
    log_pieces = lax.all_gather(prefix_log[None], "seq", axis=0, tiled=True)
    shard_ids = jnp.arange(grad_pieces.shape[0], dtype=jnp.int32)
    log_gaps = jnp.where(
        (shard_ids > own_index)[:, None], log_pieces - (prefix_log + totals)[None, :], -jnp.inf
    )
    later_grad = jnp.zeros_like(local_grad) + jnp.einsum(
        "ch,chpn->hpn", jnp.exp(log_gaps), grad_pieces, precision=highest
    )
    grad_x = jnp.einsum("hts,thp->shp", mixing, mismatch, precision=highest)
    grad_x = (
        grad_x
        + jnp.einsum("hpn,sn->shp", later_grad, b_rows, precision=highest) * ending[:, :, None]
    )
    products = jnp.einsum("thp,shp->hts", mismatch, student_x, precision=highest)
    weighted = decays * products
    grad_b = jnp.einsum("hts,tn->sn", weighted, c_rows, precision=highest)
    grad_b = grad_b + jnp.einsum(
        "shp,hpn->sn", student_x * ending[:, :, None], later_grad, precision=highest
    )
    grad_c = jnp.einsum("hts,sn->tn", weighted, b_rows, precision=highest)
    grad_c = grad_c + jnp.einsum("thp,hpn->tn", scaled_mismatch, state_in, precision=highest)
    summed_b, summed_c = (
        lax.psum_scatter(grad_b, "mp", scatter_dimension=0, tiled=True),
        lax.psum_scatter(grad_c, "mp", scatter_dimension=0, tiled=True),
    )
    return (grad_x.reshape(row_count, HQ_DEV * HEAD_WIDTH), summed_b, summed_c * c_scale)


def solution(mesh):
    in_specs = (
        P("seq", "mp"),
        P("seq", "mp"),
        P("seq", "mp"),
        P("seq", "mp"),
        P("seq", None),
        P("seq", None),
        P("seq", "mp"),
    )
    out_specs = (P("seq", "mp"), P(("seq", "mp"), None), P(("seq", "mp"), None))
    return jax.shard_map(local, mesh=mesh, in_specs=in_specs, out_specs=out_specs, check_vma=False)
```

profile of v0, /device:TPU:4, one launch (start us, length us, event | category | flops | bytes accessed | tf_op | source)
XLA Modules:
  0.0 594.7 jit_solution(6456232489600451371)
XLA Ops:
  7.2 1.4 convert_element_type.10
  8.7 0.7 all-gather.11.cloned.1.call-update
  9.5 0.8 copy.38
  10.5 1.1 copy.41
  11.7 1.9 fusion.35
  13.8 39.9 %all-gather.3 = f32[32,1,8]{2,1,0:T(1,128)S(1)} all-gather(f32[1,1,8]{2,1,0:T(1,128)S(1)} %get-tuple-element.162), channel_id=1, replica_groups=mesh['seq'=32,'mp'=8] {'seq'}, dimensions={0}, use_global_device_ids=true | all-gather | bytes 1056 | tf_op jit(solution)/shard_map/all_gather | solution.py:17
  53.7 0.9 convolution_multiply_fusion.2
  54.6 0.7 convolution_bitcast_fusion.1
  55.3 0.3 iota_compare_fusion
  55.7 35.7 %all-gather.9.cloned.1.call-done = f32[4096,128]{1,0:T(8,128)} async-done(((f32[128,128]{1,0:T(8,128)}), f32[4096,128]{1,0:T(8,128)}) %all-gather.9.cloned.1.call-update) | async-done | bytes 2097168 | tf_op jit(solution)/shard_map/all_gather | solution.py:76
  91.3 10.0 %fusion.5 = (f32[128,8]{0,1:T(8,128)S(1)}, f32[4096,128,8]{1,0,2:T(8,128)S(1)}) fusion(pred[128,4096]{0,1:T(8,128)(4,1)S(1)} %iota_compare_fusion, f32[4096,128]{1,0:T(8,128)} %all-gather.9.cloned.1.call-done, bf16[128,1024]{1,0:T(8,128)(2,1)S(1)} %copy-done), kind=kOutput, calls=%fused_computation.12 | convolution fusion | flops 6455032832 | bytes 19664896 | tf_op jit(solution)/shard_map/qkgd,nkd->qkgn/dot_general | solution.py:39
  101.4 5.7 copy-done.1
  107.1 4.0 fusion.6
  111.1 59.6 %all-gather.11.cloned.1.call-done = f32[4096,128]{1,0:T(8,128)} async-done(((f32[128,128]{1,0:T(8,128)}), f32[4096,128]{1,0:T(8,128)}) %all-gather.11.cloned.1.call-update) | async-done | bytes 2097168 | tf_op jit(solution)/shard_map/all_gather | solution.py:77
  170.7 32.2 %fusion.30 = f32[128,8,128]{2,0,1:T(8,128)S(1)} fusion(f32[4096,128]{1,0:T(8,128)} %all-gather.11.cloned.1.call-done, f32[4096,128,8]{1,0,2:T(8,128)} %copy-done.1, f32[128,8]{0,1:T(8,128)S(1)} %broadcast_maximum_fusion, pred[128,4096]{0,1:T(8,128)(4,1)S(1)} %iota_compare_fusion, f32[128,8]{0,1:T(8,128)S(1)} %fusion.6), kind=kOutput, calls=%fused_computation.40 | convolution fusion | flops 6459359232 | bytes 19931136 | tf_op jit(solution)/shard_map/qkgn,nkd->qkgd/dot_general | solution.py:48
  203.0 105.5 %all-gather.13.cloned.1.call-done = f32[256,128,128]{2,1,0:T(8,128)} async-done(((f32[8,128,128]{2,1,0:T(8,128)}), f32[256,128,128]{2,1,0:T(8,128)}) %all-gather.13.cloned.1.call-update) | async-done | bytes 16777232 | tf_op jit(solution)/shard_map/all_gather | solution.py:17
  308.5 37.8 %while.16 = (s32[]{:T(128)}, f32[8]{0:T(128)S(1)}, f32[8,128,128]{2,1,0:T(8,128)S(1)}, s32[]{:T(128)}, f32[32,8]{1,0:T(8,128)S(1)}, /*index=5*/f32[32,8,128,128]{3,2,1,0:T(8,128)}, s32[]{:T(128)}, s32[]{:T(128)}) while((s32[]{:T(128)}, f32[8]{0:T(128)S(1)}, f32[8,128,128]{2,1,0:T(8,128)S(1)}, s32[]{:T(128)}, ...), condition=%wide.region_2.3_spmd.clone, body=%wide.region_1.2_spmd.clone.sunk | while | flops 524316 | bytes 1573139 | solution.py:26
  308.5 1.2 fusion.91
  309.7 1.2 fusion.91
  310.9 1.2 fusion.91
  312.2 1.2 fusion.91
  313.4 1.2 fusion.91
  314.6 1.2 fusion.91
  315.8 1.2 fusion.91
  317.1 1.2 fusion.91
  318.3 1.2 fusion.91
  319.5 1.2 fusion.91
  320.7 1.2 fusion.91
  321.9 1.2 fusion.91
  323.2 1.2 fusion.91
  324.4 1.2 fusion.91
  325.6 1.2 fusion.91
  326.8 1.2 fusion.91
  328.0 1.2 fusion.91
  329.3 1.2 fusion.91
  330.5 1.2 fusion.91
  331.7 1.2 fusion.91
  332.9 1.2 fusion.91
  334.2 1.2 fusion.91
  335.4 1.2 fusion.91
  336.6 1.2 fusion.91
  337.8 1.2 fusion.91
  339.0 1.2 fusion.91
  340.3 1.2 fusion.91
  341.5 1.2 fusion.91
  342.7 1.2 fusion.91
  343.9 1.2 fusion.91
  345.1 1.2 fusion.91
  346.3 0.6 fusion.23
  347.0 0.7 convolution_bitcast_fusion.3
  347.7 0.4 fusion.24
  348.1 0.8 convolution_add_fusion
  349.0 1.9 fusion.40
  351.0 0.6 dynamic-slice
  352.5 63.4 %all-reduce = f32[256]{0:T(256)S(1)} all-reduce(f32[256]{0:T(256)S(1)} %dynamic-update-slice), channel_id=3, replica_groups=mesh['seq'=32,'mp'=8] {'seq'}, use_global_device_ids=true, to_apply=%add | all-reduce | flops 256 | bytes 2048
  416.2 1.2 convolution_bitcast_fusion.2
  417.4 1.3 broadcast_multiply_fusion
  418.7 106.9 %all-gather.15.cloned.1.call-done = f32[256,128,128]{2,1,0:T(8,128)} async-done(((f32[8,128,128]{2,1,0:T(8,128)}), f32[256,128,128]{2,1,0:T(8,128)}) %all-gather.15.cloned.1.call-update) | async-done | bytes 16777232 | tf_op jit(solution)/shard_map/all_gather | solution.py:116
  525.6 21.8 %fusion.3 = f32[8,1,128,128]{3,1,2,0:T(1,128)S(1)} fusion(f32[32,8,1,1]{0,2,3,1:T(1,128)S(1)} %copy.56, f32[32,8,128,128]{3,2,1,0:T(8,128)} %bitcast.129), kind=kOutput, calls=%fused_computation.9 | convolution fusion | flops 50331648 | bytes 17302528 | tf_op jit(solution)/shard_map/ch,chpn->hpn/dot_general | solution.py:122
  547.4 1.0 convolution_bitcast_fusion.4
  548.4 0.9 convolution_add_fusion.1
  549.4 0.4 fusion.21
  549.8 1.0 copy.51
  550.7 37.1 %reduce-scatter.3.cloned.1.call-done = f32[16,128]{1,0:T(8,128)} async-done(((f32[128,128]{1,0:T(8,128)}), f32[16,128]{1,0:T(8,128)}) %reduce-scatter.3.cloned.1.call-update) | async-done | bytes 8208 | tf_op jit(solution)/shard_map/reduce_scatter | solution.py:139
  (70 shorter events, 1.8 us)
Async XLA Ops:
  7.2 84.2 %copy-start = (bf16[128,1024]{1,0:T(8,128)(2,1)S(1)}, bf16[128,1024]{1,0:T(8,128)(2,1)}, u32[]{:S(2)}) copy-start(bf16[128,1024]{1,0:T(8,128)(2,1)} %param.9) | copy-start | bytes 786436
  7.2 84.2 %all-gather.9.cloned.1.call-start = ((), (), s32[]{:S(2)}) async-start(), calls=%async_computation.2 | async-start | bytes 2162688 | tf_op jit(solution)/shard_map/all_gather | solution.py:76
  8.7 162.1 %all-gather.11.cloned.1.call-start = ((), (), s32[]{:S(2)}) async-start(), calls=%async_computation.3 | async-start | bytes 2162688 | tf_op jit(solution)/shard_map/all_gather | solution.py:77
  9.4 299.1 %all-gather.13.cloned.1.call-start = ((), (), s32[]{:S(2)}) async-start(), calls=%async_computation.6 | async-start | bytes 17301504 | tf_op jit(solution)/shard_map/all_gather | solution.py:17
  13.6 403.8 %reduce-scatter.5.cloned.1.call-start = ((), (), s32[]{:S(2)}) async-start(), calls=%async_computation.5 | async-start | bytes 73728 | tf_op jit(solution)/shard_map/reduce_scatter | solution.py:140
  101.3 5.7 copy-start.1
  111.1 235.2 %copy-start.2 = (bf16[128,128]{1,0:T(8,128)(2,1)S(1)}, bf16[128,128]{1,0:T(8,128)(2,1)}, u32[]{:S(2)}) copy-start(bf16[128,128]{1,0:T(8,128)(2,1)} %param.14) | copy-start | bytes 98308
  111.1 237.0 %copy-start.3 = (bf16[128,128]{1,0:T(8,128)(2,1)S(1)}, bf16[128,128]{1,0:T(8,128)(2,1)}, u32[]{:S(2)}) copy-start(bf16[128,128]{1,0:T(8,128)(2,1)} %param.13) | copy-start | bytes 98308
  111.1 239.9 %copy-start.4 = (u32[256]{0:T(256)S(1)}, u32[256]{0:T(256)}, u32[]{:S(2)}) copy-start(u32[256]{0:T(256)} %constant.52) | copy-start | bytes 3076
  348.9 176.7 %all-gather.15.cloned.1.call-start = ((), (), s32[]{:S(2)}) async-start(), calls=%async_computation.7 | async-start | bytes 17301504 | tf_op jit(solution)/shard_map/all_gather | solution.py:116
  350.9 236.9 %reduce-scatter.3.cloned.1.call-start = ((), (), s32[]{:S(2)}) async-start(), calls=%async_computation.4 | async-start | bytes 73728 | tf_op jit(solution)/shard_map/reduce_scatter | solution.py:139
Sparse Core Ops, SparseCore 0:
  10.8 80.4 all-gather.8
  94.1 76.5 all-gather.10
  174.1 134.3 all-gather.12
  349.0 38.3 reduce-scatter.4
  391.0 134.4 all-gather.14
  549.5 38.3 reduce-scatter.2
where the time goes:
time: 597 us; the launch traced here: 595 us
  waiting for transfers between devices  346 us (58%)
  blocking collectives  103 us (17%)
  matrix products  75.6 us (13%)
  other arithmetic  44.4 us (7%)
  between operations  15 us (3%)
  local copies, waits for them, and re-layouts  9.81 us (2%)
    all_gather x1, waiting for transfers between devices, local(): grad_pieces = lax.all_gather(local_grad[None], 'seq', axis=0, tiled=True)  107 us
    all_gather x1, waiting for transfers between devices, prefix(): pieces = jax.tree.map(lambda part: lax.all_gather(part, axis), value)  105 us
    unnamed x1, blocking collectives  63.4 us
    all_gather x1, waiting for transfers between devices, local(): value_piece = lax.all_gather(values, 'seq', axis=0, tiled=True)  59.6 us
    all_gather x1, blocking collectives, prefix(): pieces = jax.tree.map(lambda part: lax.all_gather(part, axis), value)  39.9 us
    reduce_scatter x1, waiting for transfers between devices, local(): lax.psum_scatter(grad_b, 'mp', scatter_dimension=0, tiled=True)  37.1 us
    select_n x31, other arithmetic, hop(): jnp.where(position < mine, new, old)  36.4 us
    all_gather x1, waiting for transfers between devices, local(): lax.all_gather(keys.astype(jnp.float32), 'seq', axis=0, tiled=True)  35.7 us
  transfers between devices with their start and end apart: 6, of which 5 were waited for; matrix products, arithmetic and copies ran while one was open for 10% of the time, Pallas kernels for 0%

commit v1 on v0

--- a/solution.py
+++ b/solution.py
@@ -74,7 +74,9 @@
         )
     )
     key_piece = lax.all_gather(keys.astype(jnp.float32), "seq", axis=0, tiled=True)
-    value_piece = lax.all_gather(values, "seq", axis=0, tiled=True)
+    value_piece = jnp.concatenate(
+        lax.all_to_all(jnp.stack([values] * lax.axis_size("seq")), "seq", 0, 0), axis=0
+    )
     updated = []
     for current, query_head_rows, query_pos in zip(start_state, head_sets, pos_sets):
 

time: 597 us -> 525 us (0.88)
  waiting for transfers between devices: 346 us -> 219 us
  blocking collectives: 103 us -> 144 us
  starting transfers between devices: 0.24 us -> 11.8 us
    all_gather x1 -> x0, waiting for transfers between devices: 59.6 us -> none  [local(): value_piece = lax.all_gather(values, 'seq', axis=0, tiled=True)]
    all_gather x1, blocking collectives: 39.9 us -> 80.8 us  [prefix(): pieces = jax.tree.map(lambda part: lax.all_gather(part, axis), value)]
    all_gather x1, waiting for transfers between devices: 35.7 us -> 0.02 us  [local(): lax.all_gather(keys.astype(jnp.float32), 'seq', axis=0, tiled=True)]
    all_gather x1, waiting for transfers between devices: 105 us -> 75.1 us  [prefix(): pieces = jax.tree.map(lambda part: lax.all_gather(part, axis), value)]
    all_to_all x0 -> x1, starting transfers between devices: none -> 11.6 us  [local(): lax.all_to_all(jnp.stack([values] * lax.axis_size('seq')), 'seq', 0, 0)]
  transfers between devices with their start and end apart: 6 -> 6, of which waited for: 5 -> 3; matrix products, arithmetic and copies ran while one was open for 10% -> 12% of each run, Pallas kernels for 0% -> 0%
where the time goes in v1:
time: 525 us; the launch traced here: 523 us
  waiting for transfers between devices  219 us (42%)
  blocking collectives  144 us (27%)
  matrix products  75.7 us (14%)
  other arithmetic  44.4 us (8%)
  between operations  14.7 us (3%)
  local copies, waits for them, and re-layouts  12.2 us (2%)
  starting transfers between devices  11.8 us (2%)
    all_gather x1, waiting for transfers between devices, local(): grad_pieces = lax.all_gather(local_grad[None], 'seq', axis=0, tiled=True)  107 us
    all_gather x1, blocking collectives, prefix(): pieces = jax.tree.map(lambda part: lax.all_gather(part, axis), value)  80.8 us
    all_gather x1, waiting for transfers between devices, prefix(): pieces = jax.tree.map(lambda part: lax.all_gather(part, axis), value)  75.1 us
    unnamed x1, blocking collectives  63.4 us
    reduce_scatter x1, waiting for transfers between devices, local(): lax.psum_scatter(grad_b, 'mp', scatter_dimension=0, tiled=True)  37.1 us
    select_n x31, other arithmetic, hop(): jnp.where(position < mine, new, old)  36.4 us
    dot_general x1, matrix products, attend_rows(): jnp.einsum('qkgn,nkd->qkgd', weights, value_head_rows, precision=highest)  32.3 us
    dot_general x1, matrix products, local(): jnp.einsum('ch,chpn->hpn', jnp.exp(log_gaps), grad_pieces, precision=high...  21.8 us
  transfers between devices with their start and end apart: 6, of which 3 were waited for; matrix products, arithmetic and copies ran while one was open for 12% of the time, Pallas kernels for 0%

profile of v1, /device:TPU:4, one launch (start us, length us, event | category | flops | bytes accessed | tf_op | source)
XLA Modules:
  0.0 523.2 jit_solution(4304742484922876812)
XLA Ops:
  7.2 1.4 convert_element_type.10
  8.7 1.1 copy.41
  9.8 0.8 copy.38
  10.9 2.0 fusion.28
  12.9 2.4 stack.2
  15.3 11.6 %all-to-all-start = ((f32[32,128,128]{2,1,0:T(8,128)}), f32[32,128,128]{2,1,0:T(8,128)}, u32[]{:S(2)}, u32[]{:S(2)}) async-start(f32[32,128,128]{2,1,0:T(8,128)} %stack.2), calls=%async_computation | async-start | bytes 4194304 | tf_op jit(solution)/shard_map/all_to_all | solution.py:78
  27.2 80.8 %all-gather.3 = f32[32,1,8]{2,1,0:T(1,128)S(1)} all-gather(f32[1,1,8]{2,1,0:T(1,128)S(1)} %get-tuple-element.162), channel_id=1, replica_groups=mesh['seq'=32,'mp'=8] {'seq'}, dimensions={0}, use_global_device_ids=true | all-gather | bytes 1056 | tf_op jit(solution)/shard_map/all_gather | solution.py:17
  108.0 0.9 convolution_multiply_fusion.2
  108.9 0.7 convolution_bitcast_fusion.1
  109.6 0.3 iota_compare_fusion
  110.0 10.0 %fusion.5 = (f32[128,8]{0,1:T(8,128)S(1)}, f32[4096,128,8]{1,0,2:T(8,128)S(1)}) fusion(pred[128,4096]{0,1:T(8,128)(4,1)S(1)} %iota_compare_fusion, f32[4096,128]{1,0:T(8,128)} %all-gather.8.cloned.1.call-done, bf16[128,1024]{1,0:T(8,128)(2,1)S(1)} %copy-done), kind=kOutput, calls=%fused_computation.12 | convolution fusion | flops 6455032832 | bytes 19664896 | tf_op jit(solution)/shard_map/qkgd,nkd->qkgn/dot_general | solution.py:39
  120.1 5.7 %copy-done.1 = f32[4096,128,8]{1,0,2:T(8,128)} copy-done((f32[4096,128,8]{1,0,2:T(8,128)}, f32[4096,128,8]{1,0,2:T(8,128)S(1)}, u32[]{:S(2)}) %copy-start.1) | copy-done | bytes 16777240
  125.8 4.0 fusion.6
  129.9 32.3 %fusion.25 = f32[128,8,128]{2,0,1:T(8,128)S(1)} fusion(f32[4096,128,1]{1,0,2:T(8,128)} %bitcast.14, f32[4096,128,8]{1,0,2:T(8,128)} %copy-done.1, f32[128,8]{0,1:T(8,128)S(1)} %broadcast_maximum_fusion, pred[128,4096]{0,1:T(8,128)(4,1)S(1)} %iota_compare_fusion, f32[128,8]{0,1:T(8,128)S(1)} %fusion.6), kind=kOutput, calls=%fused_computation.39 | convolution fusion | flops 6459359232 | bytes 19931136 | tf_op jit(solution)/shard_map/qkgn,nkd->qkgd/dot_general | solution.py:48
  162.1 75.1 %all-gather.10.cloned.1.call-done = f32[256,128,128]{2,1,0:T(8,128)} async-done(((f32[8,128,128]{2,1,0:T(8,128)}), f32[256,128,128]{2,1,0:T(8,128)}) %all-gather.10.cloned.1.call-update) | async-done | bytes 16777232 | tf_op jit(solution)/shard_map/all_gather | solution.py:17
  237.3 37.8 %while.16 = (s32[]{:T(128)}, f32[8]{0:T(128)S(1)}, f32[8,128,128]{2,1,0:T(8,128)S(1)}, s32[]{:T(128)}, f32[32,8]{1,0:T(8,128)S(1)}, /*index=5*/f32[32,8,128,128]{3,2,1,0:T(8,128)}, s32[]{:T(128)}, s32[]{:T(128)}) while((s32[]{:T(128)}, f32[8]{0:T(128)S(1)}, f32[8,128,128]{2,1,0:T(8,128)S(1)}, s32[]{:T(128)}, ...), condition=%wide.region_2.3_spmd.clone, body=%wide.region_1.2_spmd.clone.sunk | while | flops 524316 | bytes 1573147 | solution.py:26
  237.3 1.2 fusion.85
  238.5 1.2 fusion.85
  239.7 1.2 fusion.85
  240.9 1.2 fusion.85
  242.2 1.2 fusion.85
  243.4 1.2 fusion.85
  244.6 1.2 fusion.85
  245.8 1.2 fusion.85
  247.0 1.2 fusion.85
  248.3 1.2 fusion.85
  249.5 1.2 fusion.85
  250.7 1.2 fusion.85
  251.9 1.2 fusion.85
  253.2 1.2 fusion.85
  254.4 1.2 fusion.85
  255.6 1.2 fusion.85
  256.8 1.2 fusion.85
  258.0 1.2 fusion.85
  259.3 1.2 fusion.85
  260.5 1.2 fusion.85
  261.7 1.2 fusion.85
  262.9 1.2 fusion.85
  264.1 1.2 fusion.85
  265.4 1.2 fusion.85
  266.6 1.2 fusion.85
  267.8 1.2 fusion.85
  269.0 1.2 fusion.85
  270.3 1.2 fusion.85
  271.5 1.2 fusion.85
  272.7 1.2 fusion.85
  273.9 1.2 fusion.85
  275.1 0.6 fusion.20
  275.7 0.4 fusion.21
  276.2 0.7 convolution_bitcast_fusion.3
  276.9 0.8 convolution_add_fusion
  277.8 1.9 fusion.33
  279.8 0.6 dynamic-slice
  281.1 0.2 dynamic-update-slice
  281.3 63.4 %all-reduce = f32[256]{0:T(256)S(1)} all-reduce(f32[256]{0:T(256)S(1)} %dynamic-update-slice), channel_id=3, replica_groups=mesh['seq'=32,'mp'=8] {'seq'}, use_global_device_ids=true, to_apply=%add | all-reduce | flops 256 | bytes 2048
  345.0 1.2 convolution_bitcast_fusion.2
  346.2 1.3 broadcast_multiply_fusion
  347.5 106.9 %all-gather.12.cloned.1.call-done = f32[256,128,128]{2,1,0:T(8,128)} async-done(((f32[8,128,128]{2,1,0:T(8,128)}), f32[256,128,128]{2,1,0:T(8,128)}) %all-gather.12.cloned.1.call-update) | async-done | bytes 16777232 | tf_op jit(solution)/shard_map/all_gather | solution.py:118
  454.4 21.8 %fusion.3 = f32[8,1,128,128]{3,1,2,0:T(1,128)S(1)} fusion(f32[32,8,1,1]{0,2,3,1:T(1,128)S(1)} %copy.56, f32[32,8,128,128]{3,2,1,0:T(8,128)} %bitcast.124), kind=kOutput, calls=%fused_computation.9 | convolution fusion | flops 50331648 | bytes 17302528 | tf_op jit(solution)/shard_map/ch,chpn->hpn/dot_general | solution.py:124
  476.2 1.0 convolution_bitcast_fusion.4
  477.2 0.9 convolution_add_fusion.1
  478.2 0.4 fusion.18
  478.6 1.0 copy.51
  479.6 37.1 %reduce-scatter.3.cloned.1.call-done = f32[16,128]{1,0:T(8,128)} async-done(((f32[128,128]{1,0:T(8,128)}), f32[16,128]{1,0:T(8,128)}) %reduce-scatter.3.cloned.1.call-update) | async-done | bytes 8208 | tf_op jit(solution)/shard_map/reduce_scatter | solution.py:141
  (70 shorter events, 1.6 us)
Async XLA Ops:
  7.2 102.9 %copy-start = (bf16[128,1024]{1,0:T(8,128)(2,1)S(1)}, bf16[128,1024]{1,0:T(8,128)(2,1)}, u32[]{:S(2)}) copy-start(bf16[128,1024]{1,0:T(8,128)(2,1)} %param.9) | copy-start | bytes 786436
  7.2 102.8 %all-gather.8.cloned.1.call-start = ((), (), s32[]{:S(2)}) async-start(), calls=%async_computation.3 | async-start | bytes 2162688 | tf_op jit(solution)/shard_map/all_gather | solution.py:76
  8.7 228.6 %all-gather.10.cloned.1.call-start = ((), (), s32[]{:S(2)}) async-start(), calls=%async_computation.6 | async-start | bytes 17301504 | tf_op jit(solution)/shard_map/all_gather | solution.py:17
  15.3 114.5 %all-to-all-start = ((f32[32,128,128]{2,1,0:T(8,128)}), f32[32,128,128]{2,1,0:T(8,128)}, u32[]{:S(2)}, u32[]{:S(2)}) async-start(f32[32,128,128]{2,1,0:T(8,128)} %stack.2), calls=%async_computation | async-start | bytes 4194304 | tf_op jit(solution)/shard_map/all_to_all | solution.py:78
  27.0 319.2 %reduce-scatter.5.cloned.1.call-start = ((), (), s32[]{:S(2)}) async-start(), calls=%async_computation.5 | async-start | bytes 73728 | tf_op jit(solution)/shard_map/reduce_scatter | solution.py:142
  120.0 5.7 %copy-start.1 = (f32[4096,128,8]{1,0,2:T(8,128)}, f32[4096,128,8]{1,0,2:T(8,128)S(1)}, u32[]{:S(2)}) copy-start(f32[4096,128,8]{1,0,2:T(8,128)S(1)} %get-tuple-element.164) | copy-start | bytes 50331652
  129.8 145.3 %copy-start.2 = (bf16[128,128]{1,0:T(8,128)(2,1)S(1)}, bf16[128,128]{1,0:T(8,128)(2,1)}, u32[]{:S(2)}) copy-start(bf16[128,128]{1,0:T(8,128)(2,1)} %param.14) | copy-start | bytes 98308
  129.8 147.0 %copy-start.3 = (bf16[128,128]{1,0:T(8,128)(2,1)S(1)}, bf16[128,128]{1,0:T(8,128)(2,1)}, u32[]{:S(2)}) copy-start(bf16[128,128]{1,0:T(8,128)(2,1)} %param.13) | copy-start | bytes 98308
  129.8 150.0 %copy-start.4 = (u32[256]{0:T(256)S(1)}, u32[256]{0:T(256)}, u32[]{:S(2)}) copy-start(u32[256]{0:T(256)} %constant.52) | copy-start | bytes 3076
  277.7 176.7 %all-gather.12.cloned.1.call-start = ((), (), s32[]{:S(2)}) async-start(), calls=%async_computation.7 | async-start | bytes 17301504 | tf_op jit(solution)/shard_map/all_gather | solution.py:118
  279.7 237.0 %reduce-scatter.3.cloned.1.call-start = ((), (), s32[]{:S(2)}) async-start(), calls=%async_computation.4 | async-start | bytes 73728 | tf_op jit(solution)/shard_map/reduce_scatter | solution.py:141
Sparse Core Ops, SparseCore 0:
  10.8 87.6 all-gather.7
  101.9 135.3 all-gather.9
  277.8 38.3 reduce-scatter.4
  319.8 134.4 all-gather.11
  478.3 38.3 reduce-scatter.2
